TPU v7x, 32 devices: a whole 2x2x4 slice. The times are simulated.
32 devices in a mesh: parts: 2 (over y), seq: 4 (over z), section: 2 (over x), tp: 2 (over core).
Axes of the slice: x: 2, y: 2, z: 4, core: 2. Of those that a mesh axis runs over, the one named last changes fastest.
Arguments:
- queries: bfloat16 [2, 2048, 4096], P('section', ('parts', 'seq'), 'tp'), parts along dimension 1, may hold values from -82 to 82
- keys_values: bfloat16 [2, 2, 2048, 512], P('section', None, ('parts', 'seq'), 'tp'), parts along dimension 2, may hold values from -4 to 4
- lengths: int32 [2], P('parts'), parts along dimension 0, may hold values from 769 to 1024, as said below
Outputs:
- attended: bfloat16 [2, 2048, 4096], P('section', ('parts', 'seq'), 'tp'), parts along dimension 1
- window_cache: bfloat16 [2, 2, 4096, 512], P('section', None, ('parts', 'seq'), 'tp'), parts along dimension 2
There are 2 independent parts, one for each index of `parts`. A program takes and returns all parts, laid end to end along the dimension named above; each array names one. Nothing has to cross between parts.
Inputs may be any that keep to these rules, and one draw needn't show every extreme that they name: `lengths`: the first request's length lies in min(2048, 1024 - 256) + 1 to min(2048, 1024 - 256) + 256; the second request's length is 1024.
All inputs are finite; a program needn't handle non-finite values.
Results may differ from a plain program's by a relative error of at most 0.0077.
Values may be sent and summed in bfloat16 or wider, within the bound.
No kernel may reach another device: no remote copies, remote signals or barrier semaphores. Data moves between devices by JAX's collectives and lax.ppermute only.
A program may use at most 64 MiB of HBM per device.

v0:
```python
import math
import jax
import jax.numpy as jnp
from jax import lax
from jax.sharding import PartitionSpec as P

HD = 128
WINDOW = 2048
rope_base = 1000000.0
neg_floor = -1e30


def passed_along(x, axis, by):
    devices = lax.axis_size(axis)
    pairs = [(i, i + by) for i in range(devices) if 0 <= i + by < devices]
    return lax.ppermute(x, axis, pairs)


def rotate(field, positions):
    half_dim = field.shape[-1] // 2
    frequency = jnp.exp(
        jnp.arange(half_dim, dtype=jnp.float32) * (-2.0 * math.log(rope_base) / field.shape[-1])
    )
    angles = positions.astype(jnp.float32)[:, None] * frequency[None, :]
    cosine = jnp.cos(angles)[:, None, :]
    sine_part = jnp.sin(angles)[:, None, :]
    lower_half = field[..., :half_dim]
    upper_half = field[..., half_dim:]
    return jnp.concatenate(
        [
            lower_half * cosine - upper_half * sine_part,
            upper_half * cosine + lower_half * sine_part,
        ],
        axis=-1,
    )


def local(queries, keys_values, lengths):
    seq_len = lengths[0]
    shard_rows = queries.shape[1]
    width = keys_values.shape[-1]
    kv_heads_dev = width // HD
    heads_dev = queries.shape[-1] // HD
    group_size = heads_dev // kv_heads_dev
    seq_index = lax.axis_index("seq")
    seq_count = lax.axis_size("seq")
    first_pos = seq_index * shard_rows
    positions = first_pos + jnp.arange(shard_rows, dtype=jnp.int32)
    scale = 1.0 / math.sqrt(HD)
    rotated_q = rotate(queries[0].reshape(shard_rows, heads_dev, HD).astype(jnp.float32), positions)
    rotated_q = rotated_q.astype(jnp.bfloat16).reshape(shard_rows, kv_heads_dev, group_size, HD)
    rotated_k = rotate(
        keys_values[0, 0].reshape(shard_rows, kv_heads_dev, HD).astype(jnp.float32), positions
    )
    own_block = jnp.stack(
        [rotated_k.astype(jnp.bfloat16).reshape(shard_rows, width), keys_values[0, 1]]
    )

    def attend(state_now, kv_piece, start_pos):
        row_top, totals, numer_acc = state_now
        piece_rows = kv_piece.shape[1]
        key_pos = start_pos + jnp.arange(piece_rows, dtype=jnp.int32)
        key_rows = kv_piece[0].reshape(piece_rows, kv_heads_dev, HD)
        value_rows = kv_piece[1].reshape(piece_rows, kv_heads_dev, HD)
        scores = (
            jnp.einsum("qkgd,skd->kgqs", rotated_q, key_rows, preferred_element_type=jnp.float32)
            * scale
        )
        allowed = (key_pos[None, :] <= positions[:, None]) & (
            key_pos[None, :] > positions[:, None] - WINDOW
        )
        allowed = allowed & (key_pos[None, :] >= 0) & (key_pos[None, :] < seq_len)
        top_new = jnp.maximum(row_top, jnp.max(jnp.where(allowed, scores, neg_floor), axis=-1))
        weights = jnp.where(allowed, jnp.exp(scores - top_new[..., None]), 0.0)
        rescale = jnp.exp(row_top - top_new)
        totals = totals * rescale + jnp.sum(weights, axis=-1)
        update = jnp.einsum(
            "kgqs,skd->qkgd",
            weights.astype(jnp.bfloat16),
            value_rows,
            preferred_element_type=jnp.float32,
        )
        numer_acc = numer_acc * jnp.moveaxis(rescale, 2, 0)[..., None] + update
        return (top_new, totals, numer_acc)

    start_state = (
        jnp.full((kv_heads_dev, group_size, shard_rows), neg_floor, jnp.float32),
        jnp.zeros((kv_heads_dev, group_size, shard_rows), jnp.float32),
        jnp.zeros((shard_rows, kv_heads_dev, group_size, HD), jnp.float32),
    )
    reach_count = min(WINDOW // shard_rows, seq_count - 1)
    tail_start = first_pos - reach_count * shard_rows
    older_blocks = []
    moving = own_block
    for hop in range(reach_count):
        moving = passed_along(moving, "seq", 1)
        older_blocks.insert(0, moving)
    tail_rows = jnp.concatenate(older_blocks + [own_block], axis=1)
    piece_count = tail_rows.shape[1] // shard_rows
    limit_rows = max(1024, shard_rows)
    multiple = max(
        (
            divisor
            for divisor in range(1, piece_count + 1)
            if piece_count % divisor == 0 and divisor * shard_rows <= limit_rows
        )
    )
    key_block = multiple * shard_rows

    def key_step(blk_index, state_now):
        kv_piece = lax.dynamic_slice_in_dim(tail_rows, blk_index * key_block, key_block, 1)
        return attend(state_now, kv_piece, tail_start + blk_index * key_block)

    final_state = lax.fori_loop(0, tail_rows.shape[1] // key_block, key_step, start_state)
    row_top, totals, numer_acc = final_state
    valid = positions < seq_len
    denom = jnp.where(valid[:, None, None], jnp.moveaxis(totals, 2, 0), 1.0)
    result = jnp.where(valid[:, None, None, None], numer_acc / denom[..., None], 0.0)
    attended = result.astype(jnp.bfloat16).reshape(1, shard_rows, heads_dev * HD)
    slot_rows = WINDOW // seq_count
    zero_pad = jnp.zeros((2, WINDOW, width), jnp.bfloat16)
    padded_own = jnp.concatenate([zero_pad, own_block, zero_pad], axis=1)
    begin_row = jnp.clip(seq_len - first_pos, 0, WINDOW + shard_rows)
    outbox = lax.dynamic_slice_in_dim(padded_own, begin_row, WINDOW, 1)
    received = lax.all_to_all(outbox, "seq", split_axis=1, concat_axis=1, tiled=True)
    window_cache = (
        received.reshape(2, seq_count, slot_rows, width)
        .astype(jnp.float32)
        .sum(axis=1)
        .astype(jnp.bfloat16)
    )
    return (attended, window_cache[None])


def solution(mesh):
    return jax.shard_map(
        local,
        mesh=mesh,
        in_specs=(
            P("section", ("parts", "seq"), "tp"),
            P("section", None, ("parts", "seq"), "tp"),
            P("parts"),
        ),
        out_specs=(
            P("section", ("parts", "seq"), "tp"),
            P("section", None, ("parts", "seq"), "tp"),
        ),
        check_vma=False,
    )
```

profile of v0, /device:TPU:20, one launch (start us, length us, event | category | flops | bytes accessed | tf_op | source)
XLA Modules:
  0.0 137.0 jit_solution(13391435506342000637)
XLA Ops:
  0.6 1.0 slice_convert_fusion
  1.6 0.1 copy.62
  1.8 0.1 copy.61
  1.9 0.3 multiply_cosine_fusion
  2.3 0.7 pad_maximum_fusion
  3.0 3.5 %collective-permute-start = (bf16[2,256,256]{1,2,0:T(8,128)(2,1)}, bf16[2,256,256]{1,2,0:T(8,128)(2,1)}, u32[]{:S(2)}, u32[]{:S(2)}) collective-permute-start(bf16[2,256,256]{1,2,0:T(8,128)(2,1)} %pad_maximum_fusion), channel_id=1, source_target_pairs={{0,4},{4,8},{8,12},{1,5},{5,9},{9,13},{2,6},{6,10},{10,14},{3,7},{... | collective-permute-start | bytes 786440 | tf_op jit(solution)/shard_map/ppermute | solution.py:16
  6.5 1.1 copy.53
  8.3 1.1 broadcast_in_dim.84
  9.4 30.1 %fusion.9 = bf16[2,2048,256]{2,0,1:T(2,128)(2,1)} fusion(s32[]{:T(128)S(6)} %min.4, bf16[2,2048,256]{2,0,1:T(2,128)(2,1)S(1)} %broadcast_in_dim.84, bf16[2,256,256]{2,0,1:T(2,128)(2,1)S(1)} %copy.53), kind=kLoop, calls=%fused_computation.13 | loop fusion | flops 2097152 | bytes 4456452 | tf_op jit(solution)/shard_map/concatenate | solution.py:122
  39.5 4.7 %all-to-all-start = ((bf16[2,2048,256]{2,0,1:T(2,128)(2,1)}), bf16[2,2048,256]{2,0,1:T(2,128)(2,1)S(1)}, u32[]{:S(2)}, u32[]{:S(2)}) async-start(bf16[2,2048,256]{2,0,1:T(2,128)(2,1)} %fusion.9), calls=%async_computation | async-start | bytes 4194304 | tf_op jit(solution)/shard_map/all_to_all | solution.py:125
  44.2 0.8 copy.50
  45.0 0.7 copy.48
  45.7 0.2 convert_bitcast_fusion
  46.0 0.4 copy.65
  46.4 0.0 copy-start.1
  46.4 0.7 fusion.28
  47.1 0.0 collective-permute-done
  47.1 3.4 %collective-permute-start.1 = (bf16[2,256,256]{1,2,0:T(8,128)(2,1)}, bf16[2,256,256]{1,2,0:T(8,128)(2,1)S(1)}, u32[]{:S(2)}, u32[]{:S(2)}) collective-permute-start(bf16[2,256,256]{1,2,0:T(8,128)(2,1)} %collective-permute-done), channel_id=1, source_target_pairs={{0,4},{4,8},{8,12},{1,5},{5,9},{9,13},{2,6},{6,10},{10,14},{3,7},{... | collective-permute-start | bytes 786440 | tf_op jit(solution)/shard_map/ppermute | solution.py:16
  50.5 1.4 subtract_convert_fusion
  51.9 43.8 %collective-permute-done.1 = bf16[2,256,256]{1,2,0:T(8,128)(2,1)S(1)} collective-permute-done((bf16[2,256,256]{1,2,0:T(8,128)(2,1)}, bf16[2,256,256]{1,2,0:T(8,128)(2,1)S(1)}, u32[]{:S(2)}, u32[]{:S(2)}) %collective-permute-start.1) | collective-permute-done | bytes 262176 | tf_op jit(solution)/shard_map/ppermute | solution.py:16
  95.7 2.1 %collective-permute-start.2 = (bf16[2,256,256]{1,2,0:T(8,128)(2,1)S(1)}, bf16[2,256,256]{1,2,0:T(8,128)(2,1)S(1)}, u32[]{:S(2)}, u32[]{:S(2)}) collective-permute-start(bf16[2,256,256]{1,2,0:T(8,128)(2,1)S(1)} %collective-permute-done.1), channel_id=1, source_target_pairs={{0,4},{4,8},{8,12},{1,5},{5,9},{9,13},{2,6},{6,10},{10,14},{3,7},{... | collective-permute-start | bytes 786440 | tf_op jit(solution)/shard_map/ppermute | solution.py:16
  97.8 0.9 and_and_fusion
  98.7 5.7 %collective-permute-done.2 = bf16[2,256,256]{1,2,0:T(8,128)(2,1)S(1)} collective-permute-done((bf16[2,256,256]{1,2,0:T(8,128)(2,1)S(1)}, bf16[2,256,256]{1,2,0:T(8,128)(2,1)S(1)}, u32[]{:S(2)}, u32[]{:S(2)}) %collective-permute-start.2) | collective-permute-done | bytes 262176 | tf_op jit(solution)/shard_map/ppermute | solution.py:16
  104.4 1.1 maximum_maximum_fusion
  105.5 0.1 fusion.29
  105.6 7.7 %fusion = (f32[2,8,256]{2,1,0:T(8,128)S(1)}, f32[2,1024,256,8]{2,1,3,0:T(8,128)}) fusion(pred[256,1024]{0,1:T(8,128)(4,1)S(1)} %and_and_fusion, bf16[1024,2,128,1]{0,2,3,1:T(8,128)(2,1)S(1)} %bitcast.64, bf16[256,2,8,64]{3,0,2,1:T(8,128)(2,1)S(1)} %bitcast.63, bf16[256,2,8,64]{3,0,2,1:T(8,128)(2,1)S(1)} %bitcast.62), kind=kOutput, calls=%fused_computation.2 | convolution fusion | flops 1088417792 | bytes 18628608 | tf_op jit(solution)/shard_map/while/body/eval_jaxpr/qkgd,skd->kgqs/dot_general | solution.py:66
  113.3 9.1 %fusion.3 = f32[2,8,256]{2,1,0:T(8,128)S(1)} fusion(f32[2,1024,256,8]{2,1,3,0:T(8,128)} %get-tuple-element.57, f32[2,8,256]{2,1,0:T(8,128)S(1)} %get-tuple-element.53, pred[256,1024]{0,1:T(8,128)(4,1)S(1)} %and_and_fusion), kind=kLoop, calls=%fused_computation.5 | loop fusion | flops 16773120 | bytes 17072128 | tf_op jit(solution)/shard_map/while/body/eval_jaxpr/reduce_sum | solution.py:76
  122.4 9.4 %fusion.12 = bf16[256,2,8,128]{0,3,2,1:T(8,128)(2,1)S(1)} fusion(bf16[1024,2,128,1]{0,2,3,1:T(8,128)(2,1)S(1)} %bitcast.72, f32[2,1024,256,8]{2,1,3,0:T(8,128)} %get-tuple-element.57, f32[2,8,256]{2,1,0:T(8,128)S(1)} %get-tuple-element.53, pred[256,1024]{0,1:T(8,128)(4,1)S(1)} %and_and_fusion, f32[256,2,8]{0,2,1:T(8,128)S(1)} %fusion.19, ...), kind=kOutput, calls=%fused_computation.17 | convolution fusion | flops 1092616192 | bytes 18661632 | tf_op jit(solution)/shard_map/while/body/eval_jaxpr/kgqs,skd->qkgd/dot_general | solution.py:77
  131.8 1.4 %copy.54 = bf16[1,256,2048]{2,1,0:T(8,128)(2,1)} copy(bf16[1,256,2048]{1,2,0:T(8,128)(2,1)S(1)} %bitcast.70) | data formatting | bytes 2097152
  133.2 0.0 all-to-all-done
  133.2 2.9 %reduce_sum.26 = bf16[2,512,256]{2,0,1:T(2,128)(2,1)S(1)} reduce(bf16[2,4,512,256]{3,0,2,1:T(2,128)(2,1)S(1)} %bitcast.61, bf16[]{:T(256)} %constant.50.clone.1), dimensions={1}, to_apply=%region_2.0 | reduce | flops 786432 | bytes 2621442 | tf_op jit(solution)/shard_map/reduce_sum | solution.py:129
  136.2 0.9 copy.55
  (15 shorter events, 0.1 us)
Async XLA Ops:
  3.0 44.1 %collective-permute-start = (bf16[2,256,256]{1,2,0:T(8,128)(2,1)}, bf16[2,256,256]{1,2,0:T(8,128)(2,1)}, u32[]{:S(2)}, u32[]{:S(2)}) collective-permute-start(bf16[2,256,256]{1,2,0:T(8,128)(2,1)} %pad_maximum_fusion), channel_id=1, source_target_pairs={{0,4},{4,8},{8,12},{1,5},{5,9},{9,13},{2,6},{6,10},{10,14},{3,7},{... | collective-permute-start | bytes 786440 | tf_op jit(solution)/shard_map/ppermute | solution.py:16
  39.5 6.2 %copy-start = (bf16[1,256,2048]{2,1,0:T(8,128)(2,1)S(1)}, bf16[1,256,2048]{2,1,0:T(8,128)(2,1)}, u32[]{:S(2)}) copy-start(bf16[1,256,2048]{2,1,0:T(8,128)(2,1)} %param.3) | copy-start | bytes 3145732
  39.5 93.7 %all-to-all-start = ((bf16[2,2048,256]{2,0,1:T(2,128)(2,1)}), bf16[2,2048,256]{2,0,1:T(2,128)(2,1)S(1)}, u32[]{:S(2)}, u32[]{:S(2)}) async-start(bf16[2,2048,256]{2,0,1:T(2,128)(2,1)} %fusion.9), calls=%async_computation | async-start | bytes 4194304 | tf_op jit(solution)/shard_map/all_to_all | solution.py:125
  46.4 4.1 %copy-start.1 = (f32[256,64]{1,0:T(8,128)S(1)}, f32[256,64]{1,0:T(8,128)}, u32[]{:S(2)}) copy-start(f32[256,64]{1,0:T(8,128)} %copy.50) | copy-start | bytes 196612
  46.4 4.1 %copy-start.2 = (f32[256,64]{1,0:T(8,128)S(1)}, f32[256,64]{1,0:T(8,128)}, u32[]{:S(2)}) copy-start(f32[256,64]{1,0:T(8,128)} %copy.48) | copy-start | bytes 196612
  47.1 48.6 %collective-permute-start.1 = (bf16[2,256,256]{1,2,0:T(8,128)(2,1)}, bf16[2,256,256]{1,2,0:T(8,128)(2,1)S(1)}, u32[]{:S(2)}, u32[]{:S(2)}) collective-permute-start(bf16[2,256,256]{1,2,0:T(8,128)(2,1)} %collective-permute-done), channel_id=1, source_target_pairs={{0,4},{4,8},{8,12},{1,5},{5,9},{9,13},{2,6},{6,10},{10,14},{3,7},{... | collective-permute-start | bytes 786440 | tf_op jit(solution)/shard_map/ppermute | solution.py:16
  95.7 8.7 %collective-permute-start.2 = (bf16[2,256,256]{1,2,0:T(8,128)(2,1)S(1)}, bf16[2,256,256]{1,2,0:T(8,128)(2,1)S(1)}, u32[]{:S(2)}, u32[]{:S(2)}) collective-permute-start(bf16[2,256,256]{1,2,0:T(8,128)(2,1)S(1)} %collective-permute-done.1), channel_id=1, source_target_pairs={{0,4},{4,8},{8,12},{1,5},{5,9},{9,13},{2,6},{6,10},{10,14},{3,7},{... | collective-permute-start | bytes 786440 | tf_op jit(solution)/shard_map/ppermute | solution.py:16
where the time goes:
time: 137 us
  waiting for transfers between devices  49.5 us (36%)
  other arithmetic  47.8 us (35%)
  matrix products  17.1 us (12%)
  starting transfers between devices  13.7 us (10%)
  local copies, waits for them, and re-layouts  7.42 us (5%)
  between operations  1.53 us (1%)
    ppermute x3, waiting for transfers between devices, passed_along(): return lax.ppermute(x, axis, pairs)  49.5 us
    concatenate x1, other arithmetic, local(): padded_own = jnp.concatenate([zero_pad, own_block, zero_pad], axis=1)  30.1 us
    dot_general x1, matrix products, attend(): jnp.einsum('kgqs,skd->qkgd', weights.astype(jnp.bfloat16), value_rows, pr...  9.41 us
    reduce_sum x1, other arithmetic, attend(): totals = totals * rescale + jnp.sum(weights, axis=-1)  9.12 us
    ppermute x3, starting transfers between devices, passed_along(): return lax.ppermute(x, axis, pairs)  8.94 us
    dot_general x1, matrix products, attend(): jnp.einsum('qkgd,skd->kgqs', rotated_q, key_rows, preferred_element_type=...  7.66 us
    all_to_all x1, starting transfers between devices, local(): lax.all_to_all(outbox, 'seq', split_axis=1, concat_axis=1, tiled=True)  4.73 us
    reduce_sum x1, other arithmetic, local(): window_cache = received.reshape(2, seq_count, slot_rows, width).astype(jn...  2.93 us
  transfers between devices with their start and end apart: 4, of which 2 were waited for; matrix products, arithmetic and copies ran while one was open for 48% of the time, Pallas kernels for 0%

commit v1 on v0

--- a/solution.py
+++ b/solution.py
@@ -122,7 +122,10 @@
     padded_own = jnp.concatenate([zero_pad, own_block, zero_pad], axis=1)
     begin_row = jnp.clip(seq_len - first_pos, 0, WINDOW + shard_rows)
     outbox = lax.dynamic_slice_in_dim(padded_own, begin_row, WINDOW, 1)
-    received = lax.all_to_all(outbox, "seq", split_axis=1, concat_axis=1, tiled=True)
+    received = jnp.concatenate(
+        lax.all_to_all(jnp.stack(jnp.split(outbox, lax.axis_size("seq"), axis=1)), "seq", 0, 0),
+        axis=1,
+    )
     window_cache = (
         received.reshape(2, seq_count, slot_rows, width)
         .astype(jnp.float32)

time: 137 us -> 111 us (0.81)
  other arithmetic: 47.8 us -> 22.8 us
    concatenate x1, other arithmetic: 30.1 us -> 5.08 us  [local(): padded_own = jnp.concatenate([zero_pad, own_block, zero_pad], axis=1)]
    reduce_sum x1, other arithmetic: 2.93 us -> 1.24 us  [local(): window_cache = received.reshape(2, seq_count, slot_rows, width).astype(jn...]
    another operation x2 -> x3, other arithmetic: 1.39 us -> 3.02 us  [the longest x1 1.59 us: local(): jnp.stack(jnp.split(outbox, lax.axis_size('seq'), axis=1))]
    unnamed x10 -> x11, local copies, waits for them, and re-layouts: 2.79 us -> 1.93 us
  transfers between devices with their start and end apart: 4 -> 4, of which waited for: 2 -> 2; matrix products, arithmetic and copies ran while one was open for 48% -> 39% of each run, Pallas kernels for 0% -> 0%
where the time goes in v1:
time: 111 us
  waiting for transfers between devices  49.5 us (45%)
  other arithmetic  22.8 us (21%)
  matrix products  17.1 us (15%)
  starting transfers between devices  13.7 us (12%)
  local copies, waits for them, and re-layouts  6.47 us (6%)
  between operations  1.54 us (1%)
    ppermute x3, waiting for transfers between devices, passed_along(): return lax.ppermute(x, axis, pairs)  49.5 us
    dot_general x1, matrix products, attend(): jnp.einsum('kgqs,skd->qkgd', weights.astype(jnp.bfloat16), value_rows, pr...  9.41 us
    reduce_sum x1, other arithmetic, attend(): totals = totals * rescale + jnp.sum(weights, axis=-1)  9.17 us
    ppermute x3, starting transfers between devices, passed_along(): return lax.ppermute(x, axis, pairs)  8.94 us
    dot_general x1, matrix products, attend(): jnp.einsum('qkgd,skd->kgqs', rotated_q, key_rows, preferred_element_type=...  7.65 us
    concatenate x1, other arithmetic, local(): padded_own = jnp.concatenate([zero_pad, own_block, zero_pad], axis=1)  5.08 us
    all_to_all x1, starting transfers between devices, local(): lax.all_to_all(jnp.stack(jnp.split(outbox, lax.axis_size('seq'), axis=1))...  4.73 us
  transfers between devices with their start and end apart: 4, of which 2 were waited for; matrix products, arithmetic and copies ran while one was open for 39% of the time, Pallas kernels for 0%

profile of v1, /device:TPU:20, one launch (start us, length us, event | category | flops | bytes accessed | tf_op | source)
XLA Modules:
  0.0 111.1 jit_solution(1542230494412357323)
XLA Ops:
  0.6 1.0 slice_convert_fusion
  1.6 0.1 copy.49
  1.8 0.1 copy.48
  1.9 0.3 multiply_cosine_fusion
  2.3 0.7 pad_maximum_fusion.1
  3.0 3.5 %collective-permute-start = (bf16[2,256,256]{1,2,0:T(8,128)(2,1)}, bf16[2,256,256]{1,2,0:T(8,128)(2,1)}, u32[]{:S(2)}, u32[]{:S(2)}) collective-permute-start(bf16[2,256,256]{1,2,0:T(8,128)(2,1)} %pad_maximum_fusion.1), channel_id=1, source_target_pairs={{0,4},{4,8},{8,12},{1,5},{5,9},{9,13},{2,6},{6,10},{10,14},{3,7},{... | collective-permute-start | bytes 786440 | tf_op jit(solution)/shard_map/ppermute | solution.py:16
  6.5 1.1 copy.41
  8.3 0.1 broadcast_in_dim.84
  8.4 5.1 %fusion.9 = bf16[2,2048,256]{2,1,0:T(8,128)(2,1)S(1)} fusion(s32[]{:T(128)S(6)} %min.4, bf16[2,2048,256]{2,1,0:T(8,128)(2,1)S(1)} %broadcast_in_dim.84, bf16[2,256,256]{2,1,0:T(8,128)(2,1)S(1)} %copy.41), kind=kLoop, calls=%fused_computation.13 | loop fusion | flops 6291456 | bytes 4456452 | tf_op jit(solution)/shard_map/concatenate | solution.py:122
  13.5 0.1 slice_bitcast_fusion.3
  13.6 1.6 %pad_maximum_fusion = bf16[4,2,512,256]{3,2,1,0:T(8,128)(2,1)} fusion(bf16[1,2,512,256]{3,2,1,0:T(8,128)(2,1)S(1)} %get-tuple-element.45, bf16[1,2,512,256]{3,2,1,0:T(8,128)(2,1)S(1)} %get-tuple-element.43, bf16[1,2,512,256]{3,2,1,0:T(8,128)(2,1)S(1)} %get-tuple-element.44, bf16[1,2,512,256]{3,2,1,0:T(8,128)(2,1)S(1)} %get-tuple-element.42), kind=kLoop, calls=%fused_computation.14 | loop fusion | flops 3145728 | bytes 4194304 | tf_op jit(solution)/shard_map/stack | solution.py:126
  15.2 4.7 %all-to-all-start = ((bf16[4,2,512,256]{3,2,1,0:T(8,128)(2,1)}), bf16[4,2,512,256]{3,2,1,0:T(8,128)(2,1)S(1)}, u32[]{:S(2)}, u32[]{:S(2)}) async-start(bf16[4,2,512,256]{3,2,1,0:T(8,128)(2,1)} %pad_maximum_fusion), calls=%async_computation | async-start | bytes 4194304 | tf_op jit(solution)/shard_map/all_to_all | solution.py:126
  20.0 0.8 copy.38
  20.7 0.7 copy.36
  21.5 0.2 convert_bitcast_fusion
  21.7 0.4 copy.52
  22.1 0.0 copy-start.1
  22.2 0.7 fusion.28
  22.8 3.4 %collective-permute-start.1 = (bf16[2,256,256]{1,2,0:T(8,128)(2,1)}, bf16[2,256,256]{1,2,0:T(8,128)(2,1)S(1)}, u32[]{:S(2)}, u32[]{:S(2)}) collective-permute-start(bf16[2,256,256]{1,2,0:T(8,128)(2,1)} %collective-permute-done), channel_id=1, source_target_pairs={{0,4},{4,8},{8,12},{1,5},{5,9},{9,13},{2,6},{6,10},{10,14},{3,7},{... | collective-permute-start | bytes 786440 | tf_op jit(solution)/shard_map/ppermute | solution.py:16
  26.2 1.4 %subtract_convert_fusion = (bf16[256,16,64]{2,0,1:T(8,128)(2,1)S(1)}, bf16[256,16,64]{2,0,1:T(8,128)(2,1)S(1)}) fusion(f32[256,16,64]{2,1,0:T(8,128)S(1)} %get-tuple-element.47, f32[256,16,64]{2,1,0:T(8,128)S(1)} %get-tuple-element.46, f32[256,64]{1,0:T(8,128)S(1)} %copy-done.1, f32[256,64]{1,0:T(8,128)S(1)} %copy-done.2), kind=kLoop, calls=%fused_computation.21 | loop fusion | flops 2097152 | bytes 3276800 | tf_op jit(solution)/shard_map/convert.6
  27.6 43.8 %collective-permute-done.1 = bf16[2,256,256]{1,2,0:T(8,128)(2,1)S(1)} collective-permute-done((bf16[2,256,256]{1,2,0:T(8,128)(2,1)}, bf16[2,256,256]{1,2,0:T(8,128)(2,1)S(1)}, u32[]{:S(2)}, u32[]{:S(2)}) %collective-permute-start.1) | collective-permute-done | bytes 262176 | tf_op jit(solution)/shard_map/ppermute | solution.py:16
  71.4 2.1 %collective-permute-start.2 = (bf16[2,256,256]{1,2,0:T(8,128)(2,1)S(1)}, bf16[2,256,256]{1,2,0:T(8,128)(2,1)S(1)}, u32[]{:S(2)}, u32[]{:S(2)}) collective-permute-start(bf16[2,256,256]{1,2,0:T(8,128)(2,1)S(1)} %collective-permute-done.1), channel_id=1, source_target_pairs={{0,4},{4,8},{8,12},{1,5},{5,9},{9,13},{2,6},{6,10},{10,14},{3,7},{... | collective-permute-start | bytes 786440 | tf_op jit(solution)/shard_map/ppermute | solution.py:16
  73.5 0.9 and_and_fusion
  74.4 5.7 %collective-permute-done.2 = bf16[2,256,256]{1,2,0:T(8,128)(2,1)S(1)} collective-permute-done((bf16[2,256,256]{1,2,0:T(8,128)(2,1)S(1)}, bf16[2,256,256]{1,2,0:T(8,128)(2,1)S(1)}, u32[]{:S(2)}, u32[]{:S(2)}) %collective-permute-start.2) | collective-permute-done | bytes 262176 | tf_op jit(solution)/shard_map/ppermute | solution.py:16
  80.2 1.1 maximum_maximum_fusion
  81.2 0.9 fusion.29
  82.1 7.6 %fusion = (f32[2,8,256]{2,1,0:T(8,128)S(1)}, f32[2,1024,256,8]{2,1,3,0:T(8,128)}) fusion(pred[256,1024]{0,1:T(8,128)(4,1)S(1)} %and_and_fusion, bf16[1024,2,128,1]{0,2,3,1:T(8,128)(2,1)S(1)} %bitcast.70, bf16[256,2,8,64]{3,0,2,1:T(8,128)(2,1)S(1)} %bitcast.69, bf16[256,2,8,64]{3,0,2,1:T(8,128)(2,1)S(1)} %bitcast.68), kind=kOutput, calls=%fused_computation.2 | convolution fusion | flops 1088417792 | bytes 18628608 | tf_op jit(solution)/shard_map/while/body/eval_jaxpr/qkgd,skd->kgqs/dot_general | solution.py:66
  89.8 0.0 copy-start.3
  89.8 9.2 %fusion.3 = f32[2,8,256]{2,1,0:T(8,128)S(1)} fusion(f32[2,1024,256,8]{2,1,3,0:T(8,128)} %get-tuple-element.59, f32[2,8,256]{2,1,0:T(8,128)S(1)} %get-tuple-element.55, pred[256,1024]{0,1:T(8,128)(4,1)S(1)} %and_and_fusion), kind=kLoop, calls=%fused_computation.5 | loop fusion | flops 16773120 | bytes 17072128 | tf_op jit(solution)/shard_map/while/body/eval_jaxpr/reduce_sum | solution.py:76
  99.0 9.4 %fusion.12 = bf16[256,2,8,128]{0,3,2,1:T(8,128)(2,1)S(1)} fusion(bf16[1024,2,128,1]{0,2,3,1:T(8,128)(2,1)S(1)} %bitcast.77, f32[2,1024,256,8]{2,1,3,0:T(8,128)} %get-tuple-element.59, f32[2,8,256]{2,1,0:T(8,128)S(1)} %get-tuple-element.55, pred[256,1024]{0,1:T(8,128)(4,1)S(1)} %and_and_fusion, f32[256,2,8]{0,2,1:T(8,128)S(1)} %fusion.19, ...), kind=kOutput, calls=%fused_computation.18 | convolution fusion | flops 1092616192 | bytes 18661632 | tf_op jit(solution)/shard_map/while/body/eval_jaxpr/kgqs,skd->qkgd/dot_general | solution.py:77
  108.4 1.4 %copy.42 = bf16[1,256,2048]{2,1,0:T(8,128)(2,1)} copy(bf16[1,256,2048]{1,2,0:T(8,128)(2,1)S(1)} %bitcast.75) | data formatting | bytes 2097152
  109.8 1.2 %reduce_sum.26 = bf16[2,512,256]{2,1,0:T(8,128)(2,1)} reduce(bf16[4,2,512,256]{3,2,1,0:T(8,128)(2,1)S(1)} %all-to-all-done, bf16[]{:T(256)} %constant.50.clone.1), dimensions={0}, to_apply=%region_2.0 | reduce | flops 786432 | bytes 2621442 | tf_op jit(solution)/shard_map/reduce_sum | solution.py:132
  (18 shorter events, 0.1 us)
Async XLA Ops:
  3.0 19.8 %collective-permute-start = (bf16[2,256,256]{1,2,0:T(8,128)(2,1)}, bf16[2,256,256]{1,2,0:T(8,128)(2,1)}, u32[]{:S(2)}, u32[]{:S(2)}) collective-permute-start(bf16[2,256,256]{1,2,0:T(8,128)(2,1)} %pad_maximum_fusion.1), channel_id=1, source_target_pairs={{0,4},{4,8},{8,12},{1,5},{5,9},{9,13},{2,6},{6,10},{10,14},{3,7},{... | collective-permute-start | bytes 786440 | tf_op jit(solution)/shard_map/ppermute | solution.py:16
  15.2 6.3 %copy-start = (bf16[1,256,2048]{2,1,0:T(8,128)(2,1)S(1)}, bf16[1,256,2048]{2,1,0:T(8,128)(2,1)}, u32[]{:S(2)}) copy-start(bf16[1,256,2048]{2,1,0:T(8,128)(2,1)} %param.3) | copy-start | bytes 3145732
  15.2 94.6 %all-to-all-start = ((bf16[4,2,512,256]{3,2,1,0:T(8,128)(2,1)}), bf16[4,2,512,256]{3,2,1,0:T(8,128)(2,1)S(1)}, u32[]{:S(2)}, u32[]{:S(2)}) async-start(bf16[4,2,512,256]{3,2,1,0:T(8,128)(2,1)} %pad_maximum_fusion), calls=%async_computation | async-start | bytes 4194304 | tf_op jit(solution)/shard_map/all_to_all | solution.py:126
  22.1 4.1 %copy-start.1 = (f32[256,64]{1,0:T(8,128)S(1)}, f32[256,64]{1,0:T(8,128)}, u32[]{:S(2)}) copy-start(f32[256,64]{1,0:T(8,128)} %copy.38) | copy-start | bytes 196612
  22.1 4.1 %copy-start.2 = (f32[256,64]{1,0:T(8,128)S(1)}, f32[256,64]{1,0:T(8,128)}, u32[]{:S(2)}) copy-start(f32[256,64]{1,0:T(8,128)} %copy.36) | copy-start | bytes 196612
  22.8 48.6 %collective-permute-start.1 = (bf16[2,256,256]{1,2,0:T(8,128)(2,1)}, bf16[2,256,256]{1,2,0:T(8,128)(2,1)S(1)}, u32[]{:S(2)}, u32[]{:S(2)}) collective-permute-start(bf16[2,256,256]{1,2,0:T(8,128)(2,1)} %collective-permute-done), channel_id=1, source_target_pairs={{0,4},{4,8},{8,12},{1,5},{5,9},{9,13},{2,6},{6,10},{10,14},{3,7},{... | collective-permute-start | bytes 786440 | tf_op jit(solution)/shard_map/ppermute | solution.py:16
  71.4 8.7 %collective-permute-start.2 = (bf16[2,256,256]{1,2,0:T(8,128)(2,1)S(1)}, bf16[2,256,256]{1,2,0:T(8,128)(2,1)S(1)}, u32[]{:S(2)}, u32[]{:S(2)}) collective-permute-start(bf16[2,256,256]{1,2,0:T(8,128)(2,1)S(1)} %collective-permute-done.1), channel_id=1, source_target_pairs={{0,4},{4,8},{8,12},{1,5},{5,9},{9,13},{2,6},{6,10},{10,14},{3,7},{... | collective-permute-start | bytes 786440 | tf_op jit(solution)/shard_map/ppermute | solution.py:16
  89.8 9.2 %copy-start.3 = (bf16[1,1024,256]{1,2,0:T(8,128)(2,1)S(1)}, bf16[1,1024,256]{1,2,0:T(8,128)(2,1)}, u32[]{:S(2)}) copy-start(bf16[1,1024,256]{1,2,0:T(8,128)(2,1)} %get-tuple-element.49) | copy-start | bytes 1572868
